TPU v7x, 512 devices: a whole 4x8x8 slice. The times are simulated.
512 devices in a mesh: dp: 16 (over z, core), expert: 32 (over x, y).
Axes of the slice: x: 4, y: 8, z: 8, core: 2. Of those that a mesh axis runs over, the one named last changes fastest.
Arguments:
- out_grad: bfloat16 [65536, 1024], P(('dp', 'expert')), may hold values from -6 to 6
- hidden: bfloat16 [65536, 8, 384], P(('dp', 'expert')), may hold values from -1.5 to 1.5
- gate: bfloat16 [65536, 8], P(('dp', 'expert')), may hold values from 0.049804688 to 0.5
- route_expert: int32 [65536, 8], P(('dp', 'expert')), may hold values from 0 to 63, as said below
- route_replica: int32 [65536, 8], P(('dp', 'expert')), may hold values from 0 to 3, as said below
- slot_expert: int32 [32, 3], replicated, may hold values from 0 to 63, as said below
- down_weight: bfloat16 [32, 3, 384, 1024], P('expert')
Outputs:
- d_hidden: bfloat16 [65536, 8, 384], P(('dp', 'expert'))
- d_gate: bfloat16 [65536, 8], P(('dp', 'expert'))
- d_weight: float32 [32, 3, 384, 1024], P('expert', None, 'dp')
Inputs may be any that keep to these rules, and one draw needn't show every extreme that they name: `slot_expert`: every expert holds 1 to 4 slots: exactly 8 experts hold 4, 8 hold 2, the rest 1. `route_expert`: the 8 experts of a token differ. Of the routes of one device's 128 tokens, at most 16 go to one slot, and some slot receives exactly 16 routes from every device. route_replica is below the number of slots of the route's expert.
All inputs are finite; a program needn't handle non-finite values.
Results may differ from a plain program's by a relative error of at most 0.0029.
Values may be sent and summed in bfloat16 or wider, within the bound.
No kernel may reach another device: no remote copies, remote signals or barrier semaphores. Data moves between devices by JAX's collectives and lax.ppermute only.
A program may use at most 128 MiB of HBM per device.

v0:
```python
import jax
import jax.numpy as jnp
from jax import lax
from jax.sharding import PartitionSpec as P

EXPERTS = 64
CAP = 16
HOT = 16


def slot_of_route(experts, replicas, flat_slots):
    slot_count = flat_slots.shape[0]
    ordering = jnp.arange(slot_count, dtype=jnp.int32)
    same_expert = flat_slots[:, None] == flat_slots[None, :]
    replica_rank = jnp.sum(
        (same_expert & (ordering[None, :] < ordering[:, None])).astype(jnp.int32), axis=1
    )
    matches = (experts.reshape(-1)[:, None] == flat_slots[None, :]) & (
        replicas.reshape(-1)[:, None] == replica_rank[None, :]
    )
    return jnp.sum(jnp.where(matches, ordering[None, :], 0), axis=1)


def buffer_places(experts, replicas, flat_slots, capacity):
    destination = slot_of_route(experts, replicas, flat_slots)
    slot_count = flat_slots.shape[0]
    onehot = (destination[:, None] == jnp.arange(slot_count, dtype=jnp.int32)[None, :]).astype(
        jnp.int32
    )
    before = jnp.cumsum(onehot, axis=0) - onehot
    position = jnp.sum(before * onehot, axis=1)
    return destination * capacity + position


def route_of_place(places, length):
    route_count = places.shape[0]
    return (
        jnp.full((length,), route_count, jnp.int32)
        .at[places]
        .set(jnp.arange(route_count, dtype=jnp.int32))
    )


def per_device(out_grad, hidden, gate, route_expert, route_replica, slot_expert, down_weight):
    tok_rows, chosen_count = gate.shape
    model_width = out_grad.shape[1]
    hidden_width = hidden.shape[2]
    groups, slots = slot_expert.shape
    flat_slots = slot_expert.reshape(-1)
    capacity = CAP
    block_rows = slots * capacity
    length = groups * block_rows
    route_count = tok_rows * chosen_count
    own_index = lax.axis_index("expert")
    places = buffer_places(route_expert, route_replica, flat_slots, capacity)
    source_route = route_of_place(places, length)
    hidden_rows = jnp.concatenate(
        [hidden.reshape(route_count, hidden_width), jnp.zeros((1, hidden_width), hidden.dtype)],
        axis=0,
    )
    gate_rows = jnp.concatenate([gate.reshape(route_count), jnp.zeros((1,), gate.dtype)])
    sent_hidden = hidden_rows[source_route].reshape(groups, block_rows, hidden_width)
    sent_gate = gate_rows[source_route].reshape(groups, block_rows)
    padded_grad = jnp.concatenate([out_grad, jnp.zeros((1, model_width), out_grad.dtype)], axis=0)
    token_rows = jnp.where(source_route < route_count, source_route // chosen_count, tok_rows)
    sent_grad = padded_grad[token_rows].reshape(groups, block_rows, model_width)
    got_grad, got_hidden, got_gate = (
        lax.all_to_all(sent_grad, "expert", split_axis=0, concat_axis=0, tiled=True),
        lax.all_to_all(sent_hidden, "expert", split_axis=0, concat_axis=0, tiled=True),
        lax.all_to_all(sent_gate, "expert", split_axis=0, concat_axis=0, tiled=True),
    )
    weights = down_weight[0]
    grad_four = got_grad.reshape(groups, slots, capacity, model_width)
    hidden_four = got_hidden.reshape(groups, slots, capacity, hidden_width)
    gate_four = got_gate.reshape(groups, slots, capacity).astype(jnp.float32)[..., None]
    projected = jnp.einsum("xscd,sfd->xscf", grad_four, weights, preferred_element_type=jnp.float32)
    back_rows = (
        (gate_four * projected).astype(jnp.bfloat16).reshape(groups, block_rows, hidden_width)
    )
    back_gate = (
        jnp.sum(hidden_four.astype(jnp.float32) * projected, axis=-1)
        .astype(jnp.bfloat16)
        .reshape(groups, block_rows)
    )
    came_rows, came_gate = (
        lax.all_to_all(back_rows, "expert", split_axis=0, concat_axis=0, tiled=True),
        lax.all_to_all(back_gate, "expert", split_axis=0, concat_axis=0, tiled=True),
    )
    d_hidden = came_rows.reshape(length, hidden_width)[places].reshape(
        tok_rows, chosen_count, hidden_width
    )
    d_gate = came_gate.reshape(length)[places].reshape(tok_rows, chosen_count)
    scaled = (gate_four * hidden_four.astype(jnp.float32)).astype(jnp.bfloat16)
    partial_value = jnp.einsum(
        "xscf,xscd->sfd", scaled, grad_four, preferred_element_type=jnp.float32
    )
    dp_count = lax.axis_size("dp")
    shares = lax.all_to_all(partial_value, "dp", split_axis=1, concat_axis=0, tiled=True)
    group_sum = jnp.sum(
        shares.reshape(dp_count, slots, hidden_width // dp_count, model_width), axis=0
    )
    own_slots = lax.dynamic_slice_in_dim(flat_slots, own_index * slots, slots)
    expert_ids = jnp.arange(EXPERTS, dtype=jnp.int32)
    copies = jnp.sum((flat_slots[:, None] == expert_ids[None, :]).astype(jnp.int32), axis=0)
    is_hot = copies >= 2
    hot_rank = jnp.cumsum(is_hot.astype(jnp.int32)) - 1
    picks = own_slots[:, None] == expert_ids[None, :]
    slot_hot = jnp.any(picks & is_hot[None, :], axis=1)
    slot_rank = jnp.sum(jnp.where(picks, hot_rank[None, :], 0), axis=1)
    member = (slot_rank[:, None] == jnp.arange(HOT, dtype=jnp.int32)[None, :]) & slot_hot[:, None]
    hot_table = jnp.sum(jnp.where(member[:, :, None, None], group_sum[:, None], 0.0), axis=0)
    hot_total = lax.psum(hot_table, "expert")
    from_table = jnp.sum(jnp.where(member[:, :, None, None], hot_total[None], 0.0), axis=1)
    d_weight = jnp.where(slot_hot[:, None, None], from_table, group_sum)[None]
    return (d_hidden, d_gate, d_weight)


def solution(mesh):
    placed = (
        P(("dp", "expert"), None),
        P(("dp", "expert"), None, None),
        P(("dp", "expert"), None),
        P(("dp", "expert"), None),
        P(("dp", "expert"), None),
        P(),
        P("expert", None, None, None),
    )
    return jax.shard_map(
        per_device,
        mesh=mesh,
        in_specs=placed,
        out_specs=(
            P(("dp", "expert"), None, None),
            P(("dp", "expert"), None),
            P("expert", None, "dp", None),
        ),
        check_vma=False,
    )
```

profile of v0, /device:TPU:64, one launch (start us, length us, event | category | flops | bytes accessed | tf_op | source)
XLA Modules:
  0.0 556.7 jit_solution(8288861238006414382)
XLA Ops:
  7.2 0.9 copy.108
  8.1 0.1 reshape.210
  8.2 0.8 copy.111
  9.1 0.8 copy.109
  10.0 0.8 copy.110
  10.8 0.1 eq.109
  10.9 0.2 convert_reduce_fusion
  11.1 0.1 select_reduce_fusion.2
  11.2 27.0 %reduce-window.18 = s32[96,8,128]{2,1,0:T(8,128)S(1)} reduce-window(s32[96,8,128]{2,1,0:T(8,128)S(1)} %fusion.14, s32[]{:T(128)} %constant.20.clone.1), window={size=1x1x128 pad=0_0x0_0x127_0}, to_apply=%region_2.3 | reduce-window | flops 12484608 | bytes 786436 | tf_op jit(solution)/shard_map/reduce-window
  38.3 0.2 slice.18
  38.4 0.2 copy.112
  38.6 0.1 copy.113
  38.7 0.2 broadcast_add_fusion
  38.9 0.1 fusion.13
  39.1 0.6 copy-done.2
  39.6 4.3 scatter_custom_fusion
  44.0 9.5 %gather_fusion = bf16[1536]{0:T(1024)(128)(2,1)S(1)} fusion(bf16[1025]{0:T(1024)(128)(2,1)S(1)} %pad_maximum_fusion, s32[2048]{0:T(1024)S(1)} %get-tuple-element.28), kind=kCustom, calls=%fused_computation | custom fusion | bytes 12288 | tf_op jit(solution)/shard_map/gather | solution.py:63
  53.5 0.7 all_to_all.36
  54.2 9.9 %all-to-all-start = ((bf16[32,1,48]{2,1,0:T(2,128)(2,1)}), bf16[32,1,48]{2,1,0:T(2,128)(2,1)S(1)}, u32[]{:S(2)}, u32[]{:S(2)}) async-start(bf16[32,1,48]{2,1,0:T(2,128)(2,1)} %all_to_all.36), calls=%async_computation | async-start | bytes 32768 | tf_op jit(solution)/shard_map/all_to_all | solution.py:70
  64.1 1.2 concatenate.11
  65.3 5.3 gather_fusion.3
  70.6 3.2 all-to-all-done
  73.9 6.8 %all-to-all-start.3 = ((bf16[32,48,384]{2,1,0:T(8,128)(2,1)}), bf16[32,48,384]{2,1,0:T(8,128)(2,1)}, u32[]{:S(2)}, u32[]{:S(2)}) async-start(bf16[32,48,384]{2,1,0:T(8,128)(2,1)} %bitcast.60), calls=%async_computation.3 | async-start | bytes 2359296 | tf_op jit(solution)/shard_map/all_to_all | solution.py:69
  80.7 5.8 %gather_fusion.1 = bf16[1536,1024]{1,0:T(8,128)(2,1)} fusion(bf16[129,1024]{1,0:T(8,128)(2,1)S(1)} %concatenate.10, s32[2048]{0:T(1024)S(1)} %get-tuple-element.27), kind=kCustom, calls=%fused_computation.1 | custom fusion | bytes 6297600 | tf_op jit(solution)/shard_map/gather | solution.py:66
  86.6 25.1 %all-to-all-done.3 = bf16[32,48,384]{2,1,0:T(8,128)(2,1)} async-done(((bf16[32,48,384]{2,1,0:T(8,128)(2,1)}), bf16[32,48,384]{2,1,0:T(8,128)(2,1)}, u32[]{:S(2)}, u32[]{:S(2)}) %all-to-all-start.3) | async-done | bytes 1179680 | tf_op jit(solution)/shard_map/all_to_all | solution.py:69
  111.6 5.1 all-to-all-start.1
  116.8 0.1 copy.115
  116.9 0.7 copy.116
  117.6 73.3 %all-to-all-done.1 = bf16[32,48,1024]{2,1,0:T(8,128)(2,1)} async-done(((bf16[32,48,1024]{2,1,0:T(8,128)(2,1)}), bf16[32,48,1024]{2,1,0:T(8,128)(2,1)}, u32[]{:S(2)}, u32[]{:S(2)}) %all-to-all-start.1) | async-done | bytes 3145760 | tf_op jit(solution)/shard_map/all_to_all | solution.py:68
  190.9 4.7 fusion.6
  195.6 0.8 copy.120
  196.4 0.7 copy.121
  197.1 5.4 all-to-all-start.4
  202.6 3.8 fusion.7
  206.3 5.9 %copy.125 = f32[3,384,1024]{2,0,1:T(4,128)} copy(f32[3,384,1024]{2,1,0:T(8,128)S(1)} %fusion.7) | data formatting | bytes 9437184 | tf_op jit(solution)/shard_map/xscf,xscd->sfd/dot_general | solution.py:94
  212.2 10.0 %all-to-all-start.5 = ((f32[3,384,1024]{2,0,1:T(4,128)}), f32[3,384,1024]{2,0,1:T(4,128)}, u32[]{:S(2)}, u32[]{:S(2)}) async-start(f32[3,384,1024]{2,0,1:T(4,128)} %copy.125), calls=%async_computation.5 | async-start | bytes 12582912 | tf_op jit(solution)/shard_map/all_to_all | solution.py:98
  222.2 0.8 convert_reduce_fusion.1
  223.0 0.5 broadcast_compare_fusion
  223.5 1.4 copy.122
  224.9 1.4 reduce-window.20
  226.3 1.2 dynamic_slice.3
  227.6 1.2 copy.118
  228.8 130.7 %all-to-all-done.5 = f32[3,384,1024]{2,0,1:T(4,128)} async-done(((f32[3,384,1024]{2,0,1:T(4,128)}), f32[3,384,1024]{2,0,1:T(4,128)}, u32[]{:S(2)}, u32[]{:S(2)}) %all-to-all-start.5) | async-done | bytes 4718624 | tf_op jit(solution)/shard_map/all_to_all | solution.py:98
  359.5 9.6 %all-to-all-start.2 = ((bf16[32,48,384]{2,1,0:T(8,128)(2,1)}), bf16[32,48,384]{2,1,0:T(8,128)(2,1)S(1)}, u32[]{:S(2)}, u32[]{:S(2)}) async-start(bf16[32,48,384]{2,1,0:T(8,128)(2,1)} %bitcast.61), calls=%async_computation.2 | async-start | bytes 2359296 | tf_op jit(solution)/shard_map/all_to_all | solution.py:86
  369.2 0.9 add_reduce_fusion
  370.0 0.8 select_reduce_fusion.3
  370.9 0.8 fusion.22
  371.7 0.6 copy-done.5
  372.3 0.6 fusion.23
  372.9 5.3 reduce_sum.91
  378.2 1.2 copy.126
  379.4 2.5 select_reduce_fusion.1
  381.9 1.3 broadcast_clamp_fusion
  383.2 0.7 reduce.2
  383.8 0.8 reshape.219
  384.6 6.9 %gather_fusion.4 = bf16[1024]{0:T(1024)(128)(2,1)S(1)} fusion(bf16[1536]{0:T(1024)(128)(2,1)S(1)} %reshape.219, s32[1024]{0:T(1024)} %broadcast_clamp_fusion), kind=kCustom, calls=%fused_computation.4 | custom fusion | bytes 8192 | tf_op jit(solution)/shard_map/gather | solution.py:92
  391.5 0.7 reshape.220
  392.2 1.4 copy.128
  393.6 7.3 %all-to-all-done.2 = bf16[32,48,384]{2,1,0:T(8,128)(2,1)S(1)} async-done(((bf16[32,48,384]{2,1,0:T(8,128)(2,1)}), bf16[32,48,384]{2,1,0:T(8,128)(2,1)S(1)}, u32[]{:S(2)}, u32[]{:S(2)}) %all-to-all-start.2) | async-done | bytes 1179680 | tf_op jit(solution)/shard_map/all_to_all | solution.py:86
  401.0 5.4 gather_fusion.2
  406.4 139.3 %all-reduce.4.cloned.1.call-done = f32[16,24,1024]{2,1,0:T(8,128)} async-done(((f32[16,24,1024]{2,1,0:T(8,128)}), f32[16,24,1024]{2,1,0:T(8,128)}) %all-reduce.4.cloned.1.call-update) | async-done | bytes 1572880 | tf_op jit(solution)/shard_map/psum | solution.py:112
  545.7 1.9 select_reduce_fusion
  547.7 1.3 bitcast_select_fusion
  549.0 0.9 copy.129
  (27 shorter events, 0.4 us)
Async XLA Ops:
  7.2 183.7 %copy-start = (bf16[1,3,384,1024]{3,2,1,0:T(8,128)(2,1)S(1)}, bf16[1,3,384,1024]{3,2,1,0:T(8,128)(2,1)}, u32[]{:S(2)}) copy-start(bf16[1,3,384,1024]{3,2,1,0:T(8,128)(2,1)} %param.13) | copy-start | bytes 7077892
  10.9 27.4 %copy-start.3 = (s32[96]{0:T(128)}, s32[96]{0:T(128)S(1)}, u32[]{:S(2)}) copy-start(s32[96]{0:T(128)S(1)} %eq.109) | copy-start | bytes 1156
  39.1 0.6 copy-start.2
  54.2 19.7 %all-to-all-start = ((bf16[32,1,48]{2,1,0:T(2,128)(2,1)}), bf16[32,1,48]{2,1,0:T(2,128)(2,1)S(1)}, u32[]{:S(2)}, u32[]{:S(2)}) async-start(bf16[32,1,48]{2,1,0:T(2,128)(2,1)} %all_to_all.36), calls=%async_computation | async-start | bytes 32768 | tf_op jit(solution)/shard_map/all_to_all | solution.py:70
  70.6 10.0 %copy-start.1 = (bf16[128,1024]{1,0:T(8,128)(2,1)S(1)}, bf16[128,1024]{1,0:T(8,128)(2,1)}, u32[]{:S(2)}) copy-start(bf16[128,1024]{1,0:T(8,128)(2,1)} %param.7) | copy-start | bytes 786436
  73.9 37.8 %all-to-all-start.3 = ((bf16[32,48,384]{2,1,0:T(8,128)(2,1)}), bf16[32,48,384]{2,1,0:T(8,128)(2,1)}, u32[]{:S(2)}, u32[]{:S(2)}) async-start(bf16[32,48,384]{2,1,0:T(8,128)(2,1)} %bitcast.60), calls=%async_computation.3 | async-start | bytes 2359296 | tf_op jit(solution)/shard_map/all_to_all | solution.py:69
  111.6 79.2 %all-to-all-start.1 = ((bf16[32,48,1024]{2,1,0:T(8,128)(2,1)}), bf16[32,48,1024]{2,1,0:T(8,128)(2,1)}, u32[]{:S(2)}, u32[]{:S(2)}) async-start(bf16[32,48,1024]{2,1,0:T(8,128)(2,1)} %bitcast.59), calls=%async_computation.1 | async-start | bytes 6291456 | tf_op jit(solution)/shard_map/all_to_all | solution.py:68
  197.1 15.1 %all-to-all-start.4 = ((bf16[32,1,48]{2,1,0:T(2,128)(2,1)}), bf16[32,1,48]{2,1,0:T(2,128)(2,1)S(1)}, u32[]{:S(2)}, u32[]{:S(2)}) async-start(bf16[32,1,48]{2,1,0:T(2,128)(2,1)} %copy.121), calls=%async_computation.4 | async-start | bytes 32768 | tf_op jit(solution)/shard_map/all_to_all | solution.py:87
  212.2 147.3 %all-to-all-start.5 = ((f32[3,384,1024]{2,0,1:T(4,128)}), f32[3,384,1024]{2,0,1:T(4,128)}, u32[]{:S(2)}, u32[]{:S(2)}) async-start(f32[3,384,1024]{2,0,1:T(4,128)} %copy.125), calls=%async_computation.5 | async-start | bytes 12582912 | tf_op jit(solution)/shard_map/all_to_all | solution.py:98
  359.5 41.5 %all-to-all-start.2 = ((bf16[32,48,384]{2,1,0:T(8,128)(2,1)}), bf16[32,48,384]{2,1,0:T(8,128)(2,1)S(1)}, u32[]{:S(2)}, u32[]{:S(2)}) async-start(bf16[32,48,384]{2,1,0:T(8,128)(2,1)} %bitcast.61), calls=%async_computation.2 | async-start | bytes 2359296 | tf_op jit(solution)/shard_map/all_to_all | solution.py:86
  369.1 176.6 %all-reduce.4.cloned.1.call-start = ((), (), s32[]{:S(2)}) async-start(), calls=%async_computation.6 | async-start | bytes 3145728 | tf_op jit(solution)/shard_map/psum | solution.py:112
  371.7 0.6 copy-start.5
  401.0 144.8 %copy-start.4 = (pred[3,16]{1,0:T(4,128)(4,1)S(1)}, pred[3,16]{1,0:T(4,128)(4,1)}, u32[]{:S(2)}) copy-start(pred[3,16]{1,0:T(4,128)(4,1)} %fusion.23) | copy-start | bytes 148
  401.0 146.7 %copy-start.6 = (pred[3]{0:T(512)(128)(4,1)S(1)}, pred[3]{0:T(512)(128)(4,1)}, u32[]{:S(2)}) copy-start(pred[3]{0:T(512)(128)(4,1)} %copy-done.5) | copy-start | bytes 13
Sparse Core Ops, SparseCore 0:
  382.0 163.6 all-reduce.3
where the time goes:
time: 558 us; the launch traced here: 557 us
  waiting for transfers between devices  379 us (68%)
  local copies, waits for them, and re-layouts  61.4 us (11%)
  starting transfers between devices  46.9 us (8%)
  other arithmetic  46.5 us (8%)
  between operations  14.3 us (3%)
  matrix products  8.51 us (2%)
    psum x1, waiting for transfers between devices, per_device(): hot_total = lax.psum(hot_table, 'expert')  139 us
    all_to_all x1, waiting for transfers between devices, per_device(): lax.all_to_all(partial_value, 'dp', split_axis=1, concat_axis=0, tiled=True)  131 us
    all_to_all x1, waiting for transfers between devices, per_device(): lax.all_to_all(sent_grad, 'expert', split_axis=0, concat_axis=0, tiled=True)  73.3 us
    another operation x4, other arithmetic  28.6 us
    all_to_all x1, waiting for transfers between devices, per_device(): lax.all_to_all(sent_hidden, 'expert', split_axis=0, concat_axis=0, tiled=...  25.1 us
  transfers between devices with their start and end apart: 7, of which 6 were waited for; matrix products, arithmetic and copies ran while one was open for 11% of the time, Pallas kernels for 0%

commit v1 on v0

--- a/solution.py
+++ b/solution.py
@@ -109,7 +109,7 @@
     slot_rank = jnp.sum(jnp.where(picks, hot_rank[None, :], 0), axis=1)
     member = (slot_rank[:, None] == jnp.arange(HOT, dtype=jnp.int32)[None, :]) & slot_hot[:, None]
     hot_table = jnp.sum(jnp.where(member[:, :, None, None], group_sum[:, None], 0.0), axis=0)
-    hot_total = lax.psum(hot_table, "expert")
+    hot_total = jnp.sum(lax.all_gather(hot_table, "expert"), axis=0)
     from_table = jnp.sum(jnp.where(member[:, :, None, None], hot_total[None], 0.0), axis=1)
     d_weight = jnp.where(slot_hot[:, None, None], from_table, group_sum)[None]
     return (d_hidden, d_gate, d_weight)

time: 558 us -> 743 us (1.33)
  the two profiles are of different devices: /device:TPU:64 before, /device:TPU:1 now
where the time goes in v1:
time: 743 us; the launch traced here: 742 us
  waiting for transfers between devices  556 us (75%)
  local copies, waits for them, and re-layouts  57.7 us (8%)
  other arithmetic  57.4 us (8%)
  starting transfers between devices  48 us (6%)
  between operations  14.3 us (2%)
  matrix products  8.83 us (1%)
    all_gather x1, waiting for transfers between devices, per_device(): hot_total = jnp.sum(lax.all_gather(hot_table, 'expert'), axis=0)  287 us
    all_to_all x1, waiting for transfers between devices, per_device(): lax.all_to_all(partial_value, 'dp', split_axis=1, concat_axis=0, tiled=True)  137 us
    all_to_all x1, waiting for transfers between devices, per_device(): lax.all_to_all(sent_grad, 'expert', split_axis=0, concat_axis=0, tiled=True)  73 us
    all_to_all x1, waiting for transfers between devices, per_device(): lax.all_to_all(back_rows, 'expert', split_axis=0, concat_axis=0, tiled=True)  29 us
    another operation x4, other arithmetic  27.3 us
    all_to_all x1, waiting for transfers between devices, per_device(): lax.all_to_all(sent_hidden, 'expert', split_axis=0, concat_axis=0, tiled=...  21.9 us
    reduce_sum x1, other arithmetic, per_device(): hot_total = jnp.sum(lax.all_gather(hot_table, 'expert'), axis=0)  18.5 us
  transfers between devices with their start and end apart: 7, of which 7 were waited for; matrix products, arithmetic and copies ran while one was open for 5% of the time, Pallas kernels for 0%

profile of v1, /device:TPU:1, one launch (start us, length us, event | category | flops | bytes accessed | tf_op | source)
XLA Modules:
  0.0 742.1 jit_solution(17253268308082516138)
XLA Ops:
  7.2 0.9 copy.110
  8.1 0.1 eq.109
  8.2 0.2 convert_reduce_fusion
  8.4 0.8 copy.108
  9.2 0.1 reshape.210
  9.3 0.8 copy.109
  10.1 0.1 eq.107
  10.2 0.8 copy.111
  11.0 0.1 eq.112
  11.1 0.1 select_reduce_fusion.2
  11.2 27.0 %reduce-window.18 = s32[96,8,128]{2,1,0:T(8,128)S(1)} reduce-window(s32[96,8,128]{2,1,0:T(8,128)S(1)} %fusion.14, s32[]{:T(128)} %constant.20.clone.1), window={size=1x1x128 pad=0_0x0_0x127_0}, to_apply=%region_2.3 | reduce-window | flops 12484608 | bytes 786436 | tf_op jit(solution)/shard_map/reduce-window
  38.2 0.2 slice.18
  38.4 0.2 copy.112
  38.6 0.1 copy.113
  38.7 0.2 broadcast_add_fusion
  38.9 0.1 fusion.13
  39.1 0.6 copy-done.4
  39.6 4.3 scatter_custom_fusion
  44.0 9.5 %gather_fusion = bf16[1536]{0:T(1024)(128)(2,1)S(1)} fusion(bf16[1025]{0:T(1024)(128)(2,1)S(1)} %pad_maximum_fusion, s32[2048]{0:T(1024)S(1)} %get-tuple-element.28), kind=kCustom, calls=%fused_computation | custom fusion | bytes 12288 | tf_op jit(solution)/shard_map/gather | solution.py:63
  53.5 0.7 all_to_all.36
  54.2 10.5 %all-to-all-start = ((bf16[32,1,48]{2,1,0:T(2,128)(2,1)}), bf16[32,1,48]{2,1,0:T(2,128)(2,1)S(1)}, u32[]{:S(2)}, u32[]{:S(2)}) async-start(bf16[32,1,48]{2,1,0:T(2,128)(2,1)} %all_to_all.36), calls=%async_computation | async-start | bytes 32768 | tf_op jit(solution)/shard_map/all_to_all | solution.py:70
  64.7 1.2 concatenate.11
  65.9 5.3 gather_fusion.3
  71.2 2.1 all-to-all-done
  73.3 7.4 all-to-all-start.3
  80.7 5.8 gather_fusion.1
  86.5 21.9 %all-to-all-done.3 = bf16[32,48,384]{2,1,0:T(8,128)(2,1)} async-done(((bf16[32,48,384]{2,1,0:T(8,128)(2,1)}), bf16[32,48,384]{2,1,0:T(8,128)(2,1)}, u32[]{:S(2)}, u32[]{:S(2)}) %all-to-all-start.3) | async-done | bytes 1179680 | tf_op jit(solution)/shard_map/all_to_all | solution.py:69
  108.5 8.3 %all-to-all-start.1 = ((bf16[32,48,1024]{2,1,0:T(8,128)(2,1)}), bf16[32,48,1024]{2,1,0:T(8,128)(2,1)}, u32[]{:S(2)}, u32[]{:S(2)}) async-start(bf16[32,48,1024]{2,1,0:T(8,128)(2,1)} %bitcast.62), calls=%async_computation.1 | async-start | bytes 6291456 | tf_op jit(solution)/shard_map/all_to_all | solution.py:68
  116.8 0.1 copy.115
  117.0 73.0 %all-to-all-done.1 = bf16[32,48,1024]{2,1,0:T(8,128)(2,1)} async-done(((bf16[32,48,1024]{2,1,0:T(8,128)(2,1)}), bf16[32,48,1024]{2,1,0:T(8,128)(2,1)}, u32[]{:S(2)}, u32[]{:S(2)}) %all-to-all-start.1) | async-done | bytes 3145760 | tf_op jit(solution)/shard_map/all_to_all | solution.py:68
  190.0 3.8 fusion.7
  193.8 5.9 copy.125
  199.7 12.7 %all-to-all-start.5 = ((f32[3,384,1024]{2,0,1:T(4,128)}), f32[3,384,1024]{2,0,1:T(4,128)}, u32[]{:S(2)}, u32[]{:S(2)}) async-start(f32[3,384,1024]{2,0,1:T(4,128)} %copy.125), calls=%async_computation.5 | async-start | bytes 12582912 | tf_op jit(solution)/shard_map/all_to_all | solution.py:98
  212.3 0.2 all-gather.3.cloned.1.call-start
  212.6 0.1 convert_reduce_fusion.1
  212.8 0.1 copy.122
  212.8 0.1 reduce-window.20
  212.9 0.1 add_reduce_fusion
  213.1 0.2 fusion.22
  213.3 0.2 select_reduce_fusion.3
  213.4 0.3 copy-done.7
  213.9 136.9 %all-to-all-done.5 = f32[3,384,1024]{2,0,1:T(4,128)} async-done(((f32[3,384,1024]{2,0,1:T(4,128)}), f32[3,384,1024]{2,0,1:T(4,128)}, u32[]{:S(2)}, u32[]{:S(2)}) %all-to-all-start.5) | async-done | bytes 4718624 | tf_op jit(solution)/shard_map/all_to_all | solution.py:98
  350.8 4.5 reduce_sum.100
  355.3 0.2 copy.126
  355.5 1.8 select_reduce_fusion.1
  357.3 5.1 fusion.6
  362.5 0.7 copy.121
  363.2 5.0 all-to-all-start.4
  368.2 2.6 copy.118
  370.7 6.1 all-to-all-done.4
  376.8 3.9 all-to-all-start.2
  380.8 1.3 broadcast_clamp_fusion
  382.1 0.7 reduce.2
  382.7 0.8 reshape.219
  383.5 6.9 gather_fusion.4
  390.4 0.7 reshape.220
  391.1 1.4 copy.128
  392.5 29.0 %all-to-all-done.2 = bf16[32,48,384]{2,1,0:T(8,128)(2,1)S(1)} async-done(((bf16[32,48,384]{2,1,0:T(8,128)(2,1)}), bf16[32,48,384]{2,1,0:T(8,128)(2,1)S(1)}, u32[]{:S(2)}, u32[]{:S(2)}) %all-to-all-start.2) | async-done | bytes 1179680 | tf_op jit(solution)/shard_map/all_to_all | solution.py:86
  421.5 5.3 gather_fusion.2
  426.8 286.7 %all-gather.3.cloned.1.call-done = f32[512,24,1024]{2,1,0:T(8,128)} async-done(((f32[16,24,1024]{2,1,0:T(8,128)}), f32[512,24,1024]{2,1,0:T(8,128)}) %all-gather.3.cloned.1.call-update) | async-done | bytes 50331664 | tf_op jit(solution)/shard_map/all_gather | solution.py:112
  713.5 18.5 %reduce_sum.102 = f32[16,24,1024]{2,1,0:T(8,128)} reduce(f32[32,16,24,1024]{3,2,1,0:T(8,128)} %bitcast.60, f32[]{:T(128)} %constant.53.clone.1), dimensions={0}, to_apply=%region_13.14 | reduce | flops 12189696 | bytes 51904516 | tf_op jit(solution)/shard_map/reduce_sum | solution.py:112
  732.1 1.9 select_reduce_fusion
  734.0 0.3 bitcast_select_fusion
  734.3 0.9 copy.129
  (32 shorter events, 0.5 us)
Async XLA Ops:
  7.2 350.1 %copy-start = (bf16[1,3,384,1024]{3,2,1,0:T(8,128)(2,1)S(1)}, bf16[1,3,384,1024]{3,2,1,0:T(8,128)(2,1)}, u32[]{:S(2)}) copy-start(bf16[1,3,384,1024]{3,2,1,0:T(8,128)(2,1)} %param.13) | copy-start | bytes 7077892
  39.0 0.6 copy-start.4
  54.2 19.1 %all-to-all-start = ((bf16[32,1,48]{2,1,0:T(2,128)(2,1)}), bf16[32,1,48]{2,1,0:T(2,128)(2,1)S(1)}, u32[]{:S(2)}, u32[]{:S(2)}) async-start(bf16[32,1,48]{2,1,0:T(2,128)(2,1)} %all_to_all.36), calls=%async_computation | async-start | bytes 32768 | tf_op jit(solution)/shard_map/all_to_all | solution.py:70
  71.2 9.5 %copy-start.3 = (bf16[128,1024]{1,0:T(8,128)(2,1)S(1)}, bf16[128,1024]{1,0:T(8,128)(2,1)}, u32[]{:S(2)}) copy-start(bf16[128,1024]{1,0:T(8,128)(2,1)} %param.7) | copy-start | bytes 786436
  73.3 35.2 %all-to-all-start.3 = ((bf16[32,48,384]{2,1,0:T(8,128)(2,1)}), bf16[32,48,384]{2,1,0:T(8,128)(2,1)}, u32[]{:S(2)}, u32[]{:S(2)}) async-start(bf16[32,48,384]{2,1,0:T(8,128)(2,1)} %bitcast.63), calls=%async_computation.3 | async-start | bytes 2359296 | tf_op jit(solution)/shard_map/all_to_all | solution.py:69
  108.5 81.5 %all-to-all-start.1 = ((bf16[32,48,1024]{2,1,0:T(8,128)(2,1)}), bf16[32,48,1024]{2,1,0:T(8,128)(2,1)}, u32[]{:S(2)}, u32[]{:S(2)}) async-start(bf16[32,48,1024]{2,1,0:T(8,128)(2,1)} %bitcast.62), calls=%async_computation.1 | async-start | bytes 6291456 | tf_op jit(solution)/shard_map/all_to_all | solution.py:68
  199.7 151.1 %all-to-all-start.5 = ((f32[3,384,1024]{2,0,1:T(4,128)}), f32[3,384,1024]{2,0,1:T(4,128)}, u32[]{:S(2)}, u32[]{:S(2)}) async-start(f32[3,384,1024]{2,0,1:T(4,128)} %copy.125), calls=%async_computation.5 | async-start | bytes 12582912 | tf_op jit(solution)/shard_map/all_to_all | solution.py:98
  212.3 501.2 %all-gather.3.cloned.1.call-start = ((), (), s32[]{:S(2)}) async-start(), calls=%async_computation.6 | async-start | bytes 51904512 | tf_op jit(solution)/shard_map/all_gather | solution.py:112
  213.2 0.5 copy-start.7
  213.9 141.6 %copy-start.5 = (pred[3,16]{1,0:T(4,128)(4,1)}, pred[3,16]{1,0:T(4,128)(4,1)S(1)}, u32[]{:S(2)}) copy-start(pred[3,16]{1,0:T(4,128)(4,1)S(1)} %fusion.23) | copy-start | bytes 148
  355.3 7.1 copy-start.1
  363.2 13.6 %all-to-all-start.4 = ((bf16[32,1,48]{2,1,0:T(2,128)(2,1)}), bf16[32,1,48]{2,1,0:T(2,128)(2,1)S(1)}, u32[]{:S(2)}, u32[]{:S(2)}) async-start(bf16[32,1,48]{2,1,0:T(2,128)(2,1)} %copy.121), calls=%async_computation.4 | async-start | bytes 32768 | tf_op jit(solution)/shard_map/all_to_all | solution.py:87
  376.8 44.7 %all-to-all-start.2 = ((bf16[32,48,384]{2,1,0:T(8,128)(2,1)}), bf16[32,48,384]{2,1,0:T(8,128)(2,1)S(1)}, u32[]{:S(2)}, u32[]{:S(2)}) async-start(bf16[32,48,384]{2,1,0:T(8,128)(2,1)} %bitcast.64), calls=%async_computation.2 | async-start | bytes 2359296 | tf_op jit(solution)/shard_map/all_to_all | solution.py:86
  713.5 18.5 %copy-start.6 = (pred[3,16]{1,0:T(4,128)(4,1)S(1)}, pred[3,16]{1,0:T(4,128)(4,1)}, u32[]{:S(2)}) copy-start(pred[3,16]{1,0:T(4,128)(4,1)} %copy-done.5) | copy-start | bytes 148
  713.5 20.5 %copy-start.2 = (f32[3,24,1024]{2,0,1:T(4,128)S(1)}, f32[3,24,1024]{2,0,1:T(4,128)}, u32[]{:S(2)}) copy-start(f32[3,24,1024]{2,0,1:T(4,128)} %copy-done.1) | copy-start | bytes 884740
  713.5 20.5 %copy-start.8 = (pred[3]{0:T(512)(128)(4,1)S(1)}, pred[3]{0:T(512)(128)(4,1)}, u32[]{:S(2)}) copy-start(pred[3]{0:T(512)(128)(4,1)} %copy-done.7) | copy-start | bytes 13
Sparse Core Ops, SparseCore 0:
  357.4 356.0 all-gather.2
